TPU v7x, 128 devices: a whole 4x4x4 slice. The times are simulated.
128 devices in a mesh: dp: 32 (over x, z, core), fsdp: 4 (over y).
Axes of the slice: x: 4, y: 4, z: 4, core: 2. Of those that a mesh axis runs over, the one named last changes fastest.
Arguments:
- latents: bfloat16 [2816, 8, 8, 320], P(('dp', 'fsdp')), may hold values from -6 to 6
- noise_draw: bfloat16 [2816, 8, 8, 320], P(('dp', 'fsdp')), may hold values from -6 to 6
- timesteps: int32 [2816], P(('dp', 'fsdp')), may hold values from 0 to 999
- buckets: int32 [2816], P(('dp', 'fsdp')), may hold values from 0 to 2
- owners: int32 [2816], P(('dp', 'fsdp')), may hold values from 0 to 31, as said below
- adv_grad: bfloat16 [2816, 8, 8, 320], P(('dp', 'fsdp')), may hold values from -6 to 6
- w_down: bfloat16 [2880, 640], P('fsdp'), may hold values from -0.109375 to 0.109375
- w_up: bfloat16 [5760, 320], P('fsdp'), may hold values from -0.078125 to 0.078125
- t_down: bfloat16 [2880, 640], P('fsdp'), may hold values from -0.109375 to 0.109375
- t_up: bfloat16 [5760, 320], P('fsdp'), may hold values from -0.078125 to 0.078125
Outputs:
- student_out: bfloat16 [2816, 8, 8, 320], P(('dp', 'fsdp'))
- grad_down: float32 [2880, 640], P('fsdp')
- grad_up: float32 [5760, 320], P('fsdp')
Inputs may be any that keep to these rules, and one draw needn't show every extreme that they name: `owners`: within one index of fsdp every owner receives exactly 22 tiles; at most 2 of one device's tiles name the same owner, and on every device some owner is named exactly 2 times.
All inputs are finite; a program needn't handle non-finite values.
Results may differ from a plain program's by a relative error of at most 0.015.
Values may be sent and summed in bfloat16 or wider, within the bound.
No kernel may reach another device: no remote copies, remote signals or barrier semaphores. Data moves between devices by JAX's collectives and lax.ppermute only.
A program may use at most 320 MiB of HBM per device.

v0:
```python
import jax
import jax.numpy as jnp
from jax import lax
from jax.sharding import PartitionSpec as P

GROUPS = 32
TSTEPS = 1000


distill_weight = 2.5
norm_epsilon = 1e-05


def conv_forward(volume, kernel_rows, stride):
    in_chan = volume.shape[3]
    kernel = kernel_rows.reshape(3, 3, in_chan, kernel_rows.shape[1])
    return lax.conv_general_dilated(
        volume,
        kernel,
        (stride, stride),
        ((1, 1), (1, 1)),
        dimension_numbers=("NHWC", "HWIO", "NHWC"),
        preferred_element_type=jnp.float32,
    )


def kernel_grad(volume, cotangent, stride):
    pad_upper = 1 if stride == 1 else 0
    result_grad = lax.conv_general_dilated(
        volume,
        cotangent,
        (1, 1),
        ((1, pad_upper), (1, pad_upper)),
        rhs_dilation=(stride, stride),
        dimension_numbers=("CHWN", "IHWO", "HWNC"),
        preferred_element_type=jnp.float32,
    )
    return result_grad.reshape(9 * volume.shape[3], cotangent.shape[3])


def width_masks(buckets, tile_side):
    half_side = tile_side // 2
    tile_count = buckets.shape[0]
    columns = jnp.arange(tile_side, dtype=jnp.int32)
    full_mask = (
        columns[None, None, :, None] < (tile_side - 2 * buckets)[:, None, None, None]
    ).astype(jnp.float32)
    full_mask = jnp.broadcast_to(full_mask, (tile_count, tile_side, tile_side, 1))
    half_cols = jnp.arange(half_side, dtype=jnp.int32)
    half_mask = (
        half_cols[None, None, :, None] < (half_side - buckets)[:, None, None, None]
    ).astype(jnp.float32)
    half_mask = jnp.broadcast_to(half_mask, (tile_count, half_side, half_side, 1))
    return (full_mask, half_mask)


def group_stats(hidden, half_mask):
    tile_count, height, breadth, channels = hidden.shape
    grouped = hidden.reshape(tile_count, height * breadth, GROUPS, channels // GROUPS)
    live_weight = half_mask.reshape(tile_count, height * breadth, 1, 1)
    population = jnp.sum(live_weight, axis=(1, 3), keepdims=True) * (channels // GROUPS)
    center = jnp.sum(grouped * live_weight, axis=(1, 3), keepdims=True) / population
    spread = (
        jnp.sum(jnp.square(grouped - center) * live_weight, axis=(1, 3), keepdims=True) / population
    )
    inverse = lax.rsqrt(spread + norm_epsilon)
    normed = ((grouped - center) * inverse).reshape(hidden.shape)
    return (normed, inverse, population)


def group_back(d_norm, normed, inverse, population, half_mask):
    tile_count, height, breadth, channels = d_norm.shape
    grouped_d = d_norm.reshape(tile_count, height * breadth, GROUPS, channels // GROUPS)
    grouped_n = normed.reshape(tile_count, height * breadth, GROUPS, channels // GROUPS)
    live_weight = half_mask.reshape(tile_count, height * breadth, 1, 1)
    mean_first = jnp.sum(grouped_d, axis=(1, 3), keepdims=True) / population
    mean_second = jnp.sum(grouped_d * grouped_n, axis=(1, 3), keepdims=True) / population
    result = live_weight * inverse * (grouped_d - mean_first - grouped_n * mean_second)
    return result.reshape(d_norm.shape)


def upsample(activated):
    return jnp.repeat(jnp.repeat(activated, 2, axis=1), 2, axis=2)


def network(noisy, full_mask, half_mask, down_weight, up_weight):
    hidden = conv_forward(noisy, down_weight, 2)
    normed, inverse, population = group_stats(hidden, half_mask)
    activated = (half_mask * jax.nn.silu(normed)).astype(jnp.bfloat16)
    enlarged = upsample(activated)
    output = conv_forward(enlarged, up_weight, 1)
    student = (full_mask * (noisy.astype(jnp.float32) + output)).astype(jnp.bfloat16)
    return (student, (noisy, normed, inverse, population, activated, enlarged))


def flip_kernel(up_weight):
    up_chan = up_weight.shape[0] // 9
    out_chan = up_weight.shape[1]
    return (
        up_weight.reshape(3, 3, up_chan, out_chan)[::-1, ::-1]
        .transpose(0, 1, 3, 2)
        .reshape(9 * out_chan, up_chan)
    )


def cotangents(student, target, adversarial, full_mask, half_mask, flipped, cached, loss_scale):
    source_in, normed, inverse, population, activated, enlarged = cached
    tile_count, tile_side = (student.shape[0], student.shape[1])
    half_side = tile_side // 2
    d_out = (
        full_mask
        * (
            distill_weight * (student.astype(jnp.float32) - target.astype(jnp.float32))
            + adversarial.astype(jnp.float32)
        )
        * loss_scale
    ).astype(jnp.bfloat16)
    d_up = conv_forward(d_out, flipped, 1)
    d_up = d_up.reshape(tile_count, half_side, 2, half_side, 2, flipped.shape[1])
    d_act = jnp.sum(d_up, axis=(2, 4))
    sigmoid_n = jax.nn.sigmoid(normed)
    d_norm = half_mask * d_act * sigmoid_n * (1.0 + normed * (1.0 - sigmoid_n))
    d_hidden = group_back(d_norm, normed, inverse, population, half_mask).astype(jnp.bfloat16)
    return (d_out, d_hidden)


def ring_gather(shards, dp_count, fsdp_count):
    fsdp_at = lax.axis_index("fsdp")
    core = lax.axis_index("dp") % 2
    step = 1 - 2 * core

    def lin(d, f):
        return d * fsdp_count + f

    ring_pairs = []
    for d in range(dp_count):
        toward = -1 if d % 2 == 0 else 1
        for f in range(fsdp_count):
            ring_pairs.append((lin(d, f), lin(d, (f + toward) % fsdp_count)))
    first = lax.ppermute(shards, ("dp", "fsdp"), ring_pairs)
    halves = tuple(
        lax.dynamic_slice_in_dim(piece, core * (piece.shape[0] // 2), piece.shape[0] // 2, axis=0)
        for piece in first
    )
    second = lax.ppermute(halves, ("dp", "fsdp"), ring_pairs)
    swap_pairs = [(d, d ^ 1) for d in range(dp_count)]
    other_first, other_second = lax.ppermute((first, second), "dp", swap_pairs)
    near = (fsdp_at + step + fsdp_count) % fsdp_count
    behind = (fsdp_at - step + fsdp_count) % fsdp_count
    far = (fsdp_at + 2) % fsdp_count
    gathered = []
    for own, got, got_other, half, half_other in zip(shards, first, other_first, second, other_second):
        rows = own.shape[0]
        full = jnp.zeros((fsdp_count * rows,) + own.shape[1:], own.dtype)
        full = lax.dynamic_update_slice_in_dim(full, own, fsdp_at * rows, axis=0)
        full = lax.dynamic_update_slice_in_dim(full, got, near * rows, axis=0)
        full = lax.dynamic_update_slice_in_dim(full, got_other, behind * rows, axis=0)
        full = lax.dynamic_update_slice_in_dim(full, half, far * rows + core * (rows // 2), axis=0)
        full = lax.dynamic_update_slice_in_dim(
            full, half_other, far * rows + (1 - core) * (rows // 2), axis=0
        )
        gathered.append(full)
    return tuple(gathered)


def gather_pair(down_rows, up_rows, dp_count, fsdp_count):
    if fsdp_count != 4 or dp_count % 2 or down_rows.shape[0] % 2 or up_rows.shape[0] % 2:
        return (
            lax.all_gather(down_rows, "fsdp", axis=0, tiled=True),
            lax.all_gather(up_rows, "fsdp", axis=0, tiled=True),
        )
    return ring_gather((down_rows, up_rows), dp_count, fsdp_count)


def coordinate_pairs(dp_count, fsdp_count, moved, shift):
    sizes = {"x": dp_count // 8, "z": 4, "core": 2, "y": fsdp_count}
    pairs = []
    for d in range(dp_count):
        for f in range(fsdp_count):
            place = {"x": d // 8, "z": (d // 2) % 4, "core": d % 2, "y": f}
            place[moved] = (place[moved] + shift) % sizes[moved]
            target = (place["x"] * 8 + place["z"] * 2 + place["core"]) * fsdp_count + place["y"]
            pairs.append((d * fsdp_count + f, target))
    return pairs


def scatter_sum(parts, at, count, pairs_of, axis=0):
    total = lax.dynamic_index_in_dim(parts, at, axis=axis, keepdims=False)
    for k in range(1, count):
        sent = lax.dynamic_index_in_dim(parts, (at + k) % count, axis=axis, keepdims=False)
        got = lax.ppermute(sent.astype(jnp.bfloat16), ("dp", "fsdp"), pairs_of(k))
        total = total + got.astype(jnp.float32)
    return total


def gather_blocks(block, at, count, pairs_of):
    full = jnp.zeros((count,) + block.shape, block.dtype)
    full = lax.dynamic_update_index_in_dim(full, block, at, axis=0)
    for k in range(1, count):
        got = lax.ppermute(block, ("dp", "fsdp"), pairs_of(k))
        full = lax.dynamic_update_index_in_dim(full, got, (at - k + count) % count, axis=0)
    return full


def reduce_gradients(local_down, local_up, dp_count, fsdp_count):
    d = lax.axis_index("dp")
    at = {"x": d // 8, "z": (d // 2) % 4, "core": d % 2, "y": lax.axis_index("fsdp")}
    sizes = {"x": dp_count // 8, "z": 4, "core": 2, "y": fsdp_count}
    down_size = local_down.size // fsdp_count
    chunk = 2 * down_size // (2 * sizes["x"] * sizes["z"])
    if dp_count != 32 or fsdp_count != 4 or chunk % 2:
        shard_down = lax.psum_scatter(local_down.astype(jnp.bfloat16), "fsdp", scatter_dimension=0, tiled=True)
        shard_up = lax.psum_scatter(local_up.astype(jnp.bfloat16), "fsdp", scatter_dimension=0, tiled=True)
        return (
            lax.psum(shard_down, "dp").astype(jnp.float32),
            lax.psum(shard_up, "dp").astype(jnp.float32),
        )
    table = jnp.concatenate(
        [local_down.reshape(fsdp_count, down_size), local_up.reshape(fsdp_count, down_size)], axis=1
    ).reshape(fsdp_count, 2, sizes["x"], sizes["z"], chunk)

    def pairs(moved):
        return lambda k: coordinate_pairs(dp_count, fsdp_count, moved, k)

    halves = jnp.moveaxis(table, 1, 0)
    part = scatter_sum(halves, at["core"], 2, pairs("core"))
    colour = chunk // 2
    done = []
    for c, order in enumerate((("y", "x"), ("x", "y"))):
        piece = part[..., c * colour:(c + 1) * colour]
        left = ["y", "x", "z"]
        for name in order:
            piece = scatter_sum(piece, at[name], sizes[name], pairs(name), axis=left.index(name))
            left.remove(name)
        done.append(piece)
    part = jnp.concatenate(done, axis=-1)
    part = scatter_sum(part, at["z"], sizes["z"], pairs("z"))
    part = gather_blocks(part.astype(jnp.bfloat16), at["z"], sizes["z"], pairs("z"))
    part = gather_blocks(part, at["x"], sizes["x"], pairs("x"))
    part = gather_blocks(part, at["core"], 2, pairs("core"))
    flat = part.reshape(-1).astype(jnp.float32)
    return (
        flat[:down_size].reshape(local_down.shape[0] // fsdp_count, local_down.shape[1]),
        flat[down_size:].reshape(local_up.shape[0] // fsdp_count, local_up.shape[1]),
    )


def on_device(
    latents, noise_draw, timesteps, buckets, owners, adv_grad, w_down, w_up, t_down, t_up
):
    tile_count, tile_side = (latents.shape[0], latents.shape[1])
    dp_count = lax.axis_size("dp")
    fsdp_count = lax.axis_size("fsdp")
    full_mask, half_mask = width_masks(buckets, tile_side)
    alpha_bar = jnp.square(jnp.cos(0.5 * jnp.pi * (timesteps.astype(jnp.float32) + 0.5) / TSTEPS))
    noisy = (
        full_mask
        * (
            jnp.sqrt(alpha_bar)[:, None, None, None] * latents.astype(jnp.float32)
            + jnp.sqrt(1.0 - alpha_bar)[:, None, None, None] * noise_draw.astype(jnp.float32)
        )
    ).astype(jnp.bfloat16)
    peer_cap = max(2, (tile_count + dp_count - 1) // dp_count)
    slot_count = dp_count * peer_cap
    hit_table = (owners[:, None] == jnp.arange(dp_count, dtype=jnp.int32)[None, :]).astype(
        jnp.int32
    )
    before = jnp.cumsum(hit_table, axis=0) - hit_table
    slot_of = owners * peer_cap + jnp.sum(before * hit_table, axis=1)
    slot_hits = slot_of[None, :] == jnp.arange(slot_count, dtype=jnp.int32)[:, None]
    spread_matrix = slot_hits.astype(jnp.bfloat16)
    send_noisy = (
        jnp.dot(spread_matrix, noisy.reshape(tile_count, -1), preferred_element_type=jnp.float32)
        .astype(jnp.bfloat16)
        .reshape(dp_count, peer_cap, -1)
    )
    send_code = jnp.sum(jnp.where(slot_hits, buckets[None, :] + 1, 0), axis=1).reshape(
        dp_count, peer_cap
    )
    teacher_down, teacher_up = gather_pair(t_down, t_up, dp_count, fsdp_count)
    recv_noisy, recv_code = (
        lax.all_to_all(send_noisy, "dp", split_axis=0, concat_axis=0, tiled=True),
        lax.all_to_all(send_code, "dp", split_axis=0, concat_axis=0, tiled=True),
    )
    flat_code = recv_code.reshape(slot_count)
    live_slot = (flat_code > 0).astype(jnp.int32)
    position = jnp.cumsum(live_slot) - live_slot
    pick_hits = (live_slot[None, :] == 1) & (
        position[None, :] == jnp.arange(tile_count, dtype=jnp.int32)[:, None]
    )
    pick_matrix = pick_hits.astype(jnp.bfloat16)
    own_noisy = (
        jnp.dot(pick_matrix, recv_noisy.reshape(slot_count, -1), preferred_element_type=jnp.float32)
        .astype(jnp.bfloat16)
        .reshape(latents.shape)
    )
    own_buckets = jnp.sum(jnp.where(pick_hits, flat_code[None, :] - 1, 0), axis=1).astype(jnp.int32)
    own_full, own_half = width_masks(own_buckets, tile_side)
    student_down, student_up = gather_pair(w_down, w_up, dp_count, fsdp_count)
    student, cached = network(own_noisy, own_full, own_half, student_down, student_up)
    target, _ = network(own_noisy, own_full, own_half, teacher_down, teacher_up)
    loss_scale = jnp.float32(1.0 / (tile_count * dp_count * fsdp_count))
    flipped = flip_kernel(student_up)
    d_out, d_hidden = cotangents(
        student, target, adv_grad, own_full, own_half, flipped, cached, loss_scale
    )
    local_down = kernel_grad(cached[0], d_hidden, 2)
    local_up = kernel_grad(cached[5], d_out, 1)
    grad_down, grad_up = reduce_gradients(local_down, local_up, dp_count, fsdp_count)
    return (student, grad_down, grad_up)


def solution(mesh):
    return jax.shard_map(
        on_device,
        mesh=mesh,
        in_specs=(
            P(("dp", "fsdp"), None, None, None),
            P(("dp", "fsdp"), None, None, None),
            P(("dp", "fsdp")),
            P(("dp", "fsdp")),
            P(("dp", "fsdp")),
            P(("dp", "fsdp"), None, None, None),
            P("fsdp", None),
            P("fsdp", None),
            P("fsdp", None),
            P("fsdp", None),
        ),
        out_specs=(P(("dp", "fsdp"), None, None, None), P("fsdp", None), P("fsdp", None)),
        check_vma=False,
    )
```

profile of v0, /device:TPU:1, one launch (start us, length us, event | category | flops | bytes accessed | tf_op | source)
XLA Modules:
  0.0 388.9 jit_solution(5972140088471612123)
XLA Ops:
  8.9 9.6 %all-to-all-start = ((s32[32,1,2]{2,1,0:T(1,128)}), s32[32,1,2]{2,1,0:T(1,128)}, u32[]{:S(2)}, u32[]{:S(2)}) async-start(s32[32,1,2]{2,1,0:T(1,128)} %bitcast), calls=%async_computation | async-start | bytes 32768 | tf_op jit(solution)/shard_map/all_to_all | solution.py:283
  44.1 7.4 %all-to-all-start.1 = ((bf16[32,2,20480]{2,1,0:T(2,128)(2,1)}), bf16[32,2,20480]{2,1,0:T(2,128)(2,1)S(1)}, u32[]{:S(2)}, u32[]{:S(2)}) async-start(bf16[32,2,20480]{2,1,0:T(2,128)(2,1)} %reshape.421), calls=%async_computation.1 | async-start | bytes 5242880 | tf_op jit(solution)/shard_map/all_to_all | solution.py:282
  69.6 12.1 %collective-permute-start.1 = (bf16[720,640]{1,0:T(8,128)(2,1)}, bf16[720,640]{1,0:T(8,128)(2,1)}, u32[]{:S(2)}, u32[]{:S(2)}) collective-permute-start(bf16[720,640]{1,0:T(8,128)(2,1)} %collective-permute-done), channel_id=1, source_target_pairs={{0,4},{4,0},{8,12},{12,8},{16,20},{20,16},{24,28},{28,24},{32,36},... | collective-permute-start | bytes 2764808 | tf_op jit(solution)/shard_map/ppermute | solution.py:147
  134.7 5.3 %fusion.14 = f32[22,4,4,640]{3,0,2,1:T(8,128)S(1)} fusion(bf16[3,3,320,640]{3,2,1,0:T(8,128)(2,1)} %bitcast.109, bf16[22,8,8,320]{3,2,1,0:T(8,128)(2,1)S(1)} %reshape.423), kind=kOutput, calls=%fused_computation.45 | convolution fusion | flops 1090355200 | bytes 5488640 | tf_op jit(solution)/shard_map/conv_general_dilated | solution.py:17
  140.0 5.0 %multiply_reduce_fusion.2 = (f32[22,640]{1,0:T(8,128)S(1)}, f32[22,640]{1,0:T(8,128)S(1)}, f32[22,4,4,640]{3,0,2,1:T(8,128)S(1)}) fusion(f32[22,4]{0,1:T(4,128)S(1)} %fusion.50, f32[22,4,4,640]{3,0,2,1:T(8,128)S(1)} %fusion.14, bf16[3,3,320,640]{3,2,1,0:T(8,128)(2,1)} %bitcast.6, bf16[22,8,8,320]{3,2,1,0:T(8,128)(2,1)S(1)} %reshape.423), kind=kOutput, calls=%fused_computation.19 | convolution fusion | flops 1091228160 | bytes 6502752 | tf_op jit(solution)/shard_map/conv_general_dilated | solution.py:17
  151.8 12.6 %fusion.2 = bf16[22,8,8,320]{3,0,2,1:T(8,128)(2,1)S(1)} fusion(bf16[22,8,8,640]{3,0,2,1:T(8,128)(2,1)S(1)} %bitcast.110, bf16[3,3,640,320]{3,2,1,0:T(8,128)(2,1)} %bitcast.4, f32[22,8]{0,1:T(8,128)S(1)} %fusion.49, bf16[22,8,8,320]{3,2,1,0:T(8,128)(2,1)S(1)} %copy-done.13), kind=kOutput, calls=%fused_computation.8 | convolution fusion | flops 4363223040 | bytes 7291584 | tf_op jit(solution)/shard_map/conv_general_dilated | solution.py:17
  166.1 13.3 %multiply_convert_fusion = bf16[22,8,8,320]{3,0,2,1:T(8,128)(2,1)S(1)} fusion(bf16[22,8,8,320]{3,0,2,1:T(8,128)(2,1)S(1)} %fusion.2, bf16[22,8,8,640]{3,0,2,1:T(8,128)(2,1)S(1)} %bitcast.112, bf16[3,3,640,320]{3,2,1,0:T(8,128)(2,1)} %bitcast.9, bf16[22,8,8,320]{3,2,1,0:T(8,128)(2,1)S(1)} %copy-done.19, f32[22,8]{0,1:T(8,128)S(1)} %fusion.49, ...), kind=kOutput, calls=%fused_computation.11 | convolution fusion | flops 4367278080 | bytes 9093824 | tf_op jit(solution)/shard_map/conv_general_dilated | solution.py:17
  179.4 11.9 %fusion.56 = f32[3,3,640,320]{3,2,1,0:T(8,128)} fusion(bf16[22,8,8,640]{3,0,2,1:T(8,128)(2,1)S(1)} %bitcast.111, bf16[22,8,8,320]{3,0,2,1:T(8,128)(2,1)S(1)} %multiply_convert_fusion), kind=kOutput, calls=%fused_computation.163 | convolution fusion | flops 4361420800 | bytes 10076160 | tf_op jit(solution)/shard_map/conv_general_dilated | solution.py:29
  191.3 11.7 %fusion.55 = f32[22,8,8,640]{3,0,2,1:T(8,128)} fusion(bf16[22,8,8,320]{3,0,2,1:T(8,128)(2,1)S(1)} %multiply_convert_fusion, bf16[3,3,640,320]{3,2,1,0:T(8,128)(2,1)} %bitcast.4), kind=kOutput, calls=%fused_computation.162 | convolution fusion | flops 4361420800 | bytes 8192000 | tf_op jit(solution)/shard_map/conv_general_dilated | solution.py:17
  203.0 10.1 %concatenate.12 = f32[4,1,4,4,28800]{4,3,2,0,1:T(4,128)} reshape(f32[3,3,640,320]{3,2,1,0:T(8,128)} %fusion.56) | data formatting | bytes 14745600 | tf_op jit(solution)/shard_map/concatenate | solution.py:218
  225.7 3.6 mul.288
  229.3 7.6 %mul.289 = f32[22,4,4,640]{3,2,1,0:T(4,128)} reshape(f32[22,16,32,20]{3,2,1,0:T(8,128)} %mul.288) | data formatting | bytes 1802240 | tf_op jit(solution)/shard_map/mul | solution.py:78
  236.9 7.5 %fusion.12 = f32[3,3,320,640]{3,2,1,0:T(8,128)} fusion(bf16[22,8,8,320]{3,2,1,0:T(8,128)(2,1)S(1)} %copy-done.13, f32[22,4,4,640]{3,2,1,0:T(4,128)} %mul.289, f32[22,4,4,640]{3,0,2,1:T(8,128)S(1)} %fusion.14, f32[22,640]{1,0:T(8,128)S(1)} %copy-done.17, f32[22,640]{1,0:T(8,128)S(1)} %copy-done.18, f32[22,640]{1,0:T(8,128)S(1)} %mul.273, ...), kind=kOutput, calls=%fused_computation.43 | convolution fusion | flops 1093959680 | bytes 11202912 | tf_op jit(solution)/shard_map/conv_general_dilated | solution.py:29
  244.4 8.2 %concatenate.11 = f32[4,1,4,4,28800]{4,3,2,0,1:T(4,128)} reshape(f32[3,3,320,640]{3,2,1,0:T(8,128)} %fusion.12) | data formatting | bytes 14745600 | tf_op jit(solution)/shard_map/concatenate | solution.py:218
  252.6 6.7 %constant_dynamic-update-slice_fusion.21 = f32[4,2,4,4,28800]{4,3,2,0,1:T(4,128)} fusion(f32[4,1,4,4,28800]{4,3,2,0,1:T(4,128)} %concatenate.11), kind=kLoop, calls=%fused_computation.136 | loop fusion | bytes 14745600
  262.8 6.2 %fusion = bf16[4,4,4,28800]{3,2,1,0:T(4,128)(2,1)} fusion(f32[4,2,4,4,28800]{4,3,2,0,1:T(4,128)} %constant_dynamic-update-slice_fusion.20, s32[]{:T(128)S(6)} %select_n.248), kind=kLoop, calls=%fused_computation.4 | loop fusion | bytes 7372804 | tf_op jit(solution)/shard_map/convert_element_type | solution.py:191
  269.8 6.4 %collective-permute-done.16 = bf16[4,4,4,28800]{3,2,1,0:T(4,128)(2,1)} collective-permute-done((bf16[4,4,4,28800]{3,2,1,0:T(4,128)(2,1)}, bf16[4,4,4,28800]{3,2,1,0:T(4,128)(2,1)}, u32[]{:S(2)}, u32[]{:S(2)}) %collective-permute-start.16) | collective-permute-done | bytes 3686432 | tf_op jit(solution)/shard_map/ppermute | solution.py:191
  276.2 9.1 %bitcast_add_fusion = f32[4,4,4,28800]{3,2,1,0:T(4,128)} fusion(bf16[4,4,4,28800]{3,2,1,0:T(4,128)(2,1)} %collective-permute-done.16, f32[4,2,4,4,28800]{4,3,2,0,1:T(4,128)} %constant_dynamic-update-slice_fusion.20, s32[]{:T(128)S(6)} %select_n.246), kind=kLoop, calls=%fused_computation.2 | loop fusion | flops 3686400 | bytes 18432004 | tf_op jit(solution)/shard_map/add | solution.py:192
  285.2 5.3 %fusion.54 = (f32[4,4,4,14400]{3,2,1,0:T(4,128)S(1)}, f32[4,4,4,14400]{3,2,1,0:T(4,128)S(1)}) fusion(f32[4,4,4,28800]{3,2,1,0:T(4,128)} %bitcast_add_fusion), kind=kLoop, calls=%fused_computation.161 | loop fusion | bytes 14745600 | tf_op jit(solution)/shard_map/slice | solution.py:230
  298.9 15.1 %collective-permute-done.17 = bf16[4,4,14400]{2,1,0:T(4,128)(2,1)S(1)} collective-permute-done((bf16[4,4,14400]{2,1,0:T(4,128)(2,1)S(1)}, bf16[4,4,14400]{2,1,0:T(4,128)(2,1)S(1)}, u32[]{:S(2)}, u32[]{:S(2)}) %collective-permute-start.17) | collective-permute-done | bytes 460832 | tf_op jit(solution)/shard_map/ppermute | solution.py:191
  320.2 6.3 %collective-permute-done.25 = bf16[4,4,14400]{2,1,0:T(4,128)(2,1)S(1)} collective-permute-done((bf16[4,4,14400]{2,1,0:T(4,128)(2,1)S(1)}, bf16[4,4,14400]{2,1,0:T(4,128)(2,1)S(1)}, u32[]{:S(2)}, u32[]{:S(2)}) %collective-permute-start.25) | collective-permute-done | bytes 460832 | tf_op jit(solution)/shard_map/ppermute | solution.py:191
  354.4 4.9 %collective-permute-start.36 = (bf16[4,28800]{1,0:T(4,128)(2,1)S(1)}, bf16[4,28800]{1,0:T(4,128)(2,1)S(1)}, u32[]{:S(2)}, u32[]{:S(2)}) collective-permute-start(bf16[4,28800]{1,0:T(4,128)(2,1)S(1)} %dynamic_update_slice.116), channel_id=1, source_target_pairs={{0,64},{1,65},{2,66},{3,67},{4,68},{5,69},{6,70},{7,71},{8,72},{9,... | collective-permute-start | bytes 691208 | tf_op jit(solution)/shard_map/ppermute | solution.py:200
  365.4 10.1 %collective-permute-start.38 = (bf16[4,4,28800]{2,1,0:T(4,128)(2,1)S(1)}, bf16[4,4,28800]{2,1,0:T(4,128)(2,1)S(1)}, u32[]{:S(2)}, u32[]{:S(2)}) collective-permute-start(bf16[4,4,28800]{2,1,0:T(4,128)(2,1)S(1)} %bitcast_dynamic-update-slice_fusion.2), channel_id=1, source_target_pairs={{0,4},{1,5},{2,6},{3,7},{4,0},{5,1},{6,2},{7,3},{8,12},{9,13},{10,... | collective-permute-start | bytes 2764808 | tf_op jit(solution)/shard_map/ppermute | solution.py:200
  385.0 3.7 reshape.435
  (260 shorter events, 187.8 us)
Async XLA Ops:
  0.6 53.1 %collective-permute-start.12 = (bf16[1440,320]{0,1:T(8,128)(2,1)}, bf16[1440,320]{0,1:T(8,128)(2,1)}, u32[]{:S(2)}, u32[]{:S(2)}) collective-permute-start(bf16[1440,320]{0,1:T(8,128)(2,1)} %param.19), channel_id=1, source_target_pairs={{0,3},{1,0},{2,1},{3,2},{4,5},{5,6},{6,7},{7,4},{8,11},{9,8},{10,9... | collective-permute-start | bytes 2764808 | tf_op jit(solution)/shard_map/ppermute | solution.py:140
  2.8 53.6 %collective-permute-start.4 = (bf16[1440,320]{0,1:T(8,128)(2,1)}, bf16[1440,320]{0,1:T(8,128)(2,1)}, u32[]{:S(2)}, u32[]{:S(2)}) collective-permute-start(bf16[1440,320]{0,1:T(8,128)(2,1)} %param.17), channel_id=1, source_target_pairs={{0,3},{1,0},{2,1},{3,2},{4,5},{5,6},{6,7},{7,4},{8,11},{9,8},{10,9... | collective-permute-start | bytes 2764808 | tf_op jit(solution)/shard_map/ppermute | solution.py:140
  4.1 57.0 %collective-permute-start.8 = (bf16[720,640]{1,0:T(8,128)(2,1)}, bf16[720,640]{1,0:T(8,128)(2,1)}, u32[]{:S(2)}, u32[]{:S(2)}) collective-permute-start(bf16[720,640]{1,0:T(8,128)(2,1)} %param.18), channel_id=1, source_target_pairs={{0,3},{1,0},{2,1},{3,2},{4,5},{5,6},{6,7},{7,4},{8,11},{9,8},{10,9... | collective-permute-start | bytes 2764808 | tf_op jit(solution)/shard_map/ppermute | solution.py:140
  5.1 57.9 %collective-permute-start = (bf16[720,640]{1,0:T(8,128)(2,1)}, bf16[720,640]{1,0:T(8,128)(2,1)}, u32[]{:S(2)}, u32[]{:S(2)}) collective-permute-start(bf16[720,640]{1,0:T(8,128)(2,1)} %param.16), channel_id=1, source_target_pairs={{0,3},{1,0},{2,1},{3,2},{4,5},{5,6},{6,7},{7,4},{8,11},{9,8},{10,9... | collective-permute-start | bytes 2764808 | tf_op jit(solution)/shard_map/ppermute | solution.py:140
  8.9 35.2 %all-to-all-start = ((s32[32,1,2]{2,1,0:T(1,128)}), s32[32,1,2]{2,1,0:T(1,128)}, u32[]{:S(2)}, u32[]{:S(2)}) async-start(s32[32,1,2]{2,1,0:T(1,128)} %bitcast), calls=%async_computation | async-start | bytes 32768 | tf_op jit(solution)/shard_map/all_to_all | solution.py:283
  44.1 84.7 %all-to-all-start.1 = ((bf16[32,2,20480]{2,1,0:T(2,128)(2,1)}), bf16[32,2,20480]{2,1,0:T(2,128)(2,1)S(1)}, u32[]{:S(2)}, u32[]{:S(2)}) async-start(bf16[32,2,20480]{2,1,0:T(2,128)(2,1)} %reshape.421), calls=%async_computation.1 | async-start | bytes 5242880 | tf_op jit(solution)/shard_map/all_to_all | solution.py:282
  59.7 26.9 %collective-permute-start.13 = (bf16[1440,320]{0,1:T(8,128)(2,1)}, bf16[1440,320]{0,1:T(8,128)(2,1)}, u32[]{:S(2)}, u32[]{:S(2)}) collective-permute-start(bf16[1440,320]{0,1:T(8,128)(2,1)} %collective-permute-done.12), channel_id=1, source_target_pairs={{0,4},{4,0},{8,12},{12,8},{16,20},{20,16},{24,28},{28,24},{32,36},... | collective-permute-start | bytes 2764808 | tf_op jit(solution)/shard_map/ppermute | solution.py:147
  61.1 28.5 %collective-permute-start.5 = (bf16[1440,320]{0,1:T(8,128)(2,1)}, bf16[1440,320]{0,1:T(8,128)(2,1)}, u32[]{:S(2)}, u32[]{:S(2)}) collective-permute-start(bf16[1440,320]{0,1:T(8,128)(2,1)} %collective-permute-done.4), channel_id=1, source_target_pairs={{0,4},{4,0},{8,12},{12,8},{16,20},{20,16},{24,28},{28,24},{32,36},... | collective-permute-start | bytes 2764808 | tf_op jit(solution)/shard_map/ppermute | solution.py:147
  63.0 22.9 %collective-permute-start.10 = (bf16[360,640]{1,0:T(8,128)(2,1)}, bf16[360,640]{1,0:T(8,128)(2,1)}, u32[]{:S(2)}, u32[]{:S(2)}) collective-permute-start(bf16[360,640]{1,0:T(8,128)(2,1)} %constant_dynamic-slice_fusion.1), channel_id=1, source_target_pairs={{0,3},{1,0},{2,1},{3,2},{4,5},{5,6},{6,7},{7,4},{8,11},{9,8},{10,9... | collective-permute-start | bytes 1382408 | tf_op jit(solution)/shard_map/ppermute | solution.py:145
  67.0 44.5 %collective-permute-start.9 = (bf16[720,640]{1,0:T(8,128)(2,1)}, bf16[720,640]{1,0:T(8,128)(2,1)}, u32[]{:S(2)}, u32[]{:S(2)}) collective-permute-start(bf16[720,640]{1,0:T(8,128)(2,1)} %collective-permute-done.8), channel_id=1, source_target_pairs={{0,4},{4,0},{8,12},{12,8},{16,20},{20,16},{24,28},{28,24},{32,36},... | collective-permute-start | bytes 2764808 | tf_op jit(solution)/shard_map/ppermute | solution.py:147
  69.6 46.1 %collective-permute-start.1 = (bf16[720,640]{1,0:T(8,128)(2,1)}, bf16[720,640]{1,0:T(8,128)(2,1)}, u32[]{:S(2)}, u32[]{:S(2)}) collective-permute-start(bf16[720,640]{1,0:T(8,128)(2,1)} %collective-permute-done), channel_id=1, source_target_pairs={{0,4},{4,0},{8,12},{12,8},{16,20},{20,16},{24,28},{28,24},{32,36},... | collective-permute-start | bytes 2764808 | tf_op jit(solution)/shard_map/ppermute | solution.py:147
  85.9 20.9 %collective-permute-start.2 = (bf16[360,640]{1,0:T(8,128)(2,1)}, bf16[360,640]{1,0:T(8,128)(2,1)}, u32[]{:S(2)}, u32[]{:S(2)}) collective-permute-start(bf16[360,640]{1,0:T(8,128)(2,1)} %constant_dynamic-slice_fusion.3), channel_id=1, source_target_pairs={{0,3},{1,0},{2,1},{3,2},{4,5},{5,6},{6,7},{7,4},{8,11},{9,8},{10,9... | collective-permute-start | bytes 1382408 | tf_op jit(solution)/shard_map/ppermute | solution.py:145
  86.6 20.6 %collective-permute-start.7 = (bf16[720,320]{0,1:T(8,128)(2,1)}, bf16[720,320]{0,1:T(8,128)(2,1)}, u32[]{:S(2)}, u32[]{:S(2)}) collective-permute-start(bf16[720,320]{0,1:T(8,128)(2,1)} %collective-permute-done.6), channel_id=1, source_target_pairs={{0,4},{4,0},{8,12},{12,8},{16,20},{20,16},{24,28},{28,24},{32,36},... | collective-permute-start | bytes 1382408 | tf_op jit(solution)/shard_map/ppermute | solution.py:147
  89.6 19.9 %collective-permute-start.15 = (bf16[720,320]{0,1:T(8,128)(2,1)}, bf16[720,320]{0,1:T(8,128)(2,1)}, u32[]{:S(2)}, u32[]{:S(2)}) collective-permute-start(bf16[720,320]{0,1:T(8,128)(2,1)} %collective-permute-done.14), channel_id=1, source_target_pairs={{0,4},{4,0},{8,12},{12,8},{16,20},{20,16},{24,28},{28,24},{32,36},... | collective-permute-start | bytes 1382408 | tf_op jit(solution)/shard_map/ppermute | solution.py:147
  106.8 13.1 %collective-permute-start.11 = (bf16[360,640]{1,0:T(8,128)(2,1)}, bf16[360,640]{1,0:T(8,128)(2,1)}, u32[]{:S(2)}, u32[]{:S(2)}) collective-permute-start(bf16[360,640]{1,0:T(8,128)(2,1)} %collective-permute-done.10), channel_id=1, source_target_pairs={{0,4},{4,0},{8,12},{12,8},{16,20},{20,16},{24,28},{28,24},{32,36},... | collective-permute-start | bytes 1382408 | tf_op jit(solution)/shard_map/ppermute | solution.py:147
  107.2 14.5 %collective-permute-start.3 = (bf16[360,640]{1,0:T(8,128)(2,1)}, bf16[360,640]{1,0:T(8,128)(2,1)}, u32[]{:S(2)}, u32[]{:S(2)}) collective-permute-start(bf16[360,640]{1,0:T(8,128)(2,1)} %collective-permute-done.2), channel_id=1, source_target_pairs={{0,4},{4,0},{8,12},{12,8},{16,20},{20,16},{24,28},{28,24},{32,36},... | collective-permute-start | bytes 1382408 | tf_op jit(solution)/shard_map/ppermute | solution.py:147
  291.0 23.0 %collective-permute-start.17 = (bf16[4,4,14400]{2,1,0:T(4,128)(2,1)S(1)}, bf16[4,4,14400]{2,1,0:T(4,128)(2,1)S(1)}, u32[]{:S(2)}, u32[]{:S(2)}) collective-permute-start(bf16[4,4,14400]{2,1,0:T(4,128)(2,1)S(1)} %get-tuple-element.31), channel_id=1, source_target_pairs={{0,1},{1,2},{2,3},{3,0},{4,5},{5,6},{6,7},{7,4},{8,9},{9,10},{10,1... | collective-permute-start | bytes 1382408 | tf_op jit(solution)/shard_map/ppermute | solution.py:191
  291.1 25.7 %collective-permute-start.18 = (bf16[4,4,14400]{2,1,0:T(4,128)(2,1)S(1)}, bf16[4,4,14400]{2,1,0:T(4,128)(2,1)S(1)}, u32[]{:S(2)}, u32[]{:S(2)}) collective-permute-start(bf16[4,4,14400]{2,1,0:T(4,128)(2,1)S(1)} %get-tuple-element.33), channel_id=1, source_target_pairs={{0,2},{1,3},{2,0},{3,1},{4,6},{5,7},{6,4},{7,5},{8,10},{9,11},{10,... | collective-permute-start | bytes 1382408 | tf_op jit(solution)/shard_map/ppermute | solution.py:191
  292.5 24.3 %collective-permute-start.19 = (bf16[4,4,14400]{2,1,0:T(4,128)(2,1)S(1)}, bf16[4,4,14400]{2,1,0:T(4,128)(2,1)S(1)}, u32[]{:S(2)}, u32[]{:S(2)}) collective-permute-start(bf16[4,4,14400]{2,1,0:T(4,128)(2,1)S(1)} %get-tuple-element.32), channel_id=1, source_target_pairs={{0,3},{1,0},{2,1},{3,2},{4,7},{5,4},{6,5},{7,6},{8,11},{9,8},{10,9... | collective-permute-start | bytes 1382408 | tf_op jit(solution)/shard_map/ppermute | solution.py:191
  294.9 24.3 %collective-permute-start.23 = (bf16[4,4,14400]{2,1,0:T(4,128)(2,1)S(1)}, bf16[4,4,14400]{2,1,0:T(4,128)(2,1)S(1)}, u32[]{:S(2)}, u32[]{:S(2)}) collective-permute-start(bf16[4,4,14400]{2,1,0:T(4,128)(2,1)S(1)} %get-tuple-element.34), channel_id=1, source_target_pairs={{0,32},{1,33},{2,34},{3,35},{4,36},{5,37},{6,38},{7,39},{8,40},{9,... | collective-permute-start | bytes 1382408 | tf_op jit(solution)/shard_map/ppermute | solution.py:191
  296.5 23.7 %collective-permute-start.24 = (bf16[4,4,14400]{2,1,0:T(4,128)(2,1)S(1)}, bf16[4,4,14400]{2,1,0:T(4,128)(2,1)S(1)}, u32[]{:S(2)}, u32[]{:S(2)}) collective-permute-start(bf16[4,4,14400]{2,1,0:T(4,128)(2,1)S(1)} %get-tuple-element.36), channel_id=1, source_target_pairs={{0,64},{1,65},{2,66},{3,67},{4,68},{5,69},{6,70},{7,71},{8,72},{9,... | collective-permute-start | bytes 1382408 | tf_op jit(solution)/shard_map/ppermute | solution.py:191
  314.0 12.5 %collective-permute-start.25 = (bf16[4,4,14400]{2,1,0:T(4,128)(2,1)S(1)}, bf16[4,4,14400]{2,1,0:T(4,128)(2,1)S(1)}, u32[]{:S(2)}, u32[]{:S(2)}) collective-permute-start(bf16[4,4,14400]{2,1,0:T(4,128)(2,1)S(1)} %get-tuple-element.35), channel_id=1, source_target_pairs={{0,96},{1,97},{2,98},{3,99},{4,100},{5,101},{6,102},{7,103},{8,104... | collective-permute-start | bytes 1382408 | tf_op jit(solution)/shard_map/ppermute | solution.py:191
  317.5 12.4 %collective-permute-start.21 = (bf16[4,14400]{1,0:T(4,128)(2,1)S(1)}, bf16[4,14400]{1,0:T(4,128)(2,1)S(1)}, u32[]{:S(2)}, u32[]{:S(2)}) collective-permute-start(bf16[4,14400]{1,0:T(4,128)(2,1)S(1)} %get-tuple-element.41), channel_id=1, source_target_pairs={{0,64},{1,65},{2,66},{3,67},{4,68},{5,69},{6,70},{7,71},{8,72},{9,... | collective-permute-start | bytes 345608 | tf_op jit(solution)/shard_map/ppermute | solution.py:191
  365.4 12.2 %collective-permute-start.38 = (bf16[4,4,28800]{2,1,0:T(4,128)(2,1)S(1)}, bf16[4,4,28800]{2,1,0:T(4,128)(2,1)S(1)}, u32[]{:S(2)}, u32[]{:S(2)}) collective-permute-start(bf16[4,4,28800]{2,1,0:T(4,128)(2,1)S(1)} %bitcast_dynamic-update-slice_fusion.2), channel_id=1, source_target_pairs={{0,4},{1,5},{2,6},{3,7},{4,0},{5,1},{6,2},{7,3},{8,12},{9,13},{10,... | collective-permute-start | bytes 2764808 | tf_op jit(solution)/shard_map/ppermute | solution.py:200
  (40 other events, 275.5 us)
where the time goes:
time: 394 us; the launch traced here: 389 us
  local copies, waits for them, and re-layouts  160 us (41%)
  starting transfers between devices  83.3 us (21%)
  matrix products  71.6 us (18%)
  waiting for transfers between devices  42.6 us (11%)
  other arithmetic  29.7 us (8%)
    conv_general_dilated x5, matrix products, conv_forward(): lax.conv_general_dilated(volume, kernel, (stride, stride), ((1, 1), (1, 1...  47.9 us
    ppermute x16, waiting for transfers between devices, scatter_sum(): got = lax.ppermute(sent.astype(jnp.bfloat16), ('dp', 'fsdp'), pairs_of(k))  33.3 us
    concatenate x3, local copies, waits for them, and re-layouts, reduce_gradients(): jnp.concatenate([local_down.reshape(fsdp_count, down_size), local_up.resh...  21.8 us
    ppermute x16, starting transfers between devices, scatter_sum(): got = lax.ppermute(sent.astype(jnp.bfloat16), ('dp', 'fsdp'), pairs_of(k))  21.3 us
    conv_general_dilated x2, matrix products, kernel_grad(): lax.conv_general_dilated(volume, cotangent, (1, 1), ((1, pad_upper), (1,...  19.4 us
    ppermute x7, starting transfers between devices, gather_blocks(): got = lax.ppermute(block, ('dp', 'fsdp'), pairs_of(k))  18.9 us
    unnamed x51, local copies, waits for them, and re-layouts  17.8 us
    ppermute x8, starting transfers between devices, ring_gather(): other_first, other_second = lax.ppermute((first, second), 'dp', swap_pairs)  17.1 us
  transfers between devices with their start and end apart: 41, of which 12 were waited for; matrix products, arithmetic and copies ran while one was open for 23% of the time, Pallas kernels for 0%

commit v1 on v0

--- a/solution.py
+++ b/solution.py
@@ -160,7 +160,7 @@
             full, half_other, far * rows + (1 - core) * (rows // 2), axis=0
         )
         gathered.append(full)
-    return tuple(gathered)
+    return (tuple(gathered), second)
 
 
 def gather_pair(down_rows, up_rows, dp_count, fsdp_count):
@@ -168,8 +168,10 @@
         return (
             lax.all_gather(down_rows, "fsdp", axis=0, tiled=True),
             lax.all_gather(up_rows, "fsdp", axis=0, tiled=True),
-        )
-    return ring_gather((down_rows, up_rows), dp_count, fsdp_count)
+            (down_rows, up_rows),
+        )
+    gathered, last_hop = ring_gather((down_rows, up_rows), dp_count, fsdp_count)
+    return gathered + (last_hop,)
 
 
 def coordinate_pairs(dp_count, fsdp_count, moved, shift):
@@ -277,7 +279,6 @@
     send_code = jnp.sum(jnp.where(slot_hits, buckets[None, :] + 1, 0), axis=1).reshape(
         dp_count, peer_cap
     )
-    teacher_down, teacher_up = gather_pair(t_down, t_up, dp_count, fsdp_count)
     recv_noisy, recv_code = (
         lax.all_to_all(send_noisy, "dp", split_axis=0, concat_axis=0, tiled=True),
         lax.all_to_all(send_code, "dp", split_axis=0, concat_axis=0, tiled=True),
@@ -296,7 +297,9 @@
     )
     own_buckets = jnp.sum(jnp.where(pick_hits, flat_code[None, :] - 1, 0), axis=1).astype(jnp.int32)
     own_full, own_half = width_masks(own_buckets, tile_side)
-    student_down, student_up = gather_pair(w_down, w_up, dp_count, fsdp_count)
+    student_down, student_up, student_hop = gather_pair(w_down, w_up, dp_count, fsdp_count)
+    t_down, t_up, _ = lax.optimization_barrier((t_down, t_up, student_hop))
+    teacher_down, teacher_up, _ = gather_pair(t_down, t_up, dp_count, fsdp_count)
     student, cached = network(own_noisy, own_full, own_half, student_down, student_up)
     target, _ = network(own_noisy, own_full, own_half, teacher_down, teacher_up)
     loss_scale = jnp.float32(1.0 / (tile_count * dp_count * fsdp_count))

time: 394 us -> 388 us (0.985)
  waiting for transfers between devices: 42.6 us -> 31.2 us
    ppermute x8, starting transfers between devices: 17.1 us -> 5.2 us  [ring_gather(): other_first, other_second = lax.ppermute((first, second), 'dp', swap_pairs)]
    ppermute x16, waiting for transfers between devices: 33.3 us -> 23 us  [scatter_sum(): got = lax.ppermute(sent.astype(jnp.bfloat16), ('dp', 'fsdp'), pairs_of(k))]
    ppermute x4, starting transfers between devices: 4.57 us -> 13.5 us  [ring_gather(): first = lax.ppermute(shards, ('dp', 'fsdp'), ring_pairs)]
    ppermute x16, starting transfers between devices: 21.3 us -> 26.8 us  [scatter_sum(): got = lax.ppermute(sent.astype(jnp.bfloat16), ('dp', 'fsdp'), pairs_of(k))]
    unnamed x51 -> x38, local copies, waits for them, and re-layouts: 17.8 us -> 13.8 us
  transfers between devices with their start and end apart: 41 -> 41, of which waited for: 12 -> 13; matrix products, arithmetic and copies ran while one was open for 23% -> 30% of each run, Pallas kernels for 0% -> 0%
where the time goes in v1:
time: 388 us; the launch traced here: 383 us
  local copies, waits for them, and re-layouts  161 us (41%)
  starting transfers between devices  86 us (22%)
  matrix products  70.8 us (18%)
  other arithmetic  31.9 us (8%)
  waiting for transfers between devices  31.2 us (8%)
    conv_general_dilated x5, matrix products, conv_forward(): lax.conv_general_dilated(volume, kernel, (stride, stride), ((1, 1), (1, 1...  47.1 us
    ppermute x16, starting transfers between devices, scatter_sum(): got = lax.ppermute(sent.astype(jnp.bfloat16), ('dp', 'fsdp'), pairs_of(k))  26.8 us
    ppermute x16, waiting for transfers between devices, scatter_sum(): got = lax.ppermute(sent.astype(jnp.bfloat16), ('dp', 'fsdp'), pairs_of(k))  23 us
    concatenate x3, local copies, waits for them, and re-layouts, reduce_gradients(): jnp.concatenate([local_down.reshape(fsdp_count, down_size), local_up.resh...  22 us
    ppermute x7, starting transfers between devices, gather_blocks(): got = lax.ppermute(block, ('dp', 'fsdp'), pairs_of(k))  19.4 us
    conv_general_dilated x2, matrix products, kernel_grad(): lax.conv_general_dilated(volume, cotangent, (1, 1), ((1, pad_upper), (1,...  19.4 us
    unnamed x38, local copies, waits for them, and re-layouts  13.8 us
    ppermute x4, starting transfers between devices, ring_gather(): first = lax.ppermute(shards, ('dp', 'fsdp'), ring_pairs)  13.5 us
  transfers between devices with their start and end apart: 41, of which 13 were waited for; matrix products, arithmetic and copies ran while one was open for 30% of the time, Pallas kernels for 0%

profile of v1, /device:TPU:1, one launch (start us, length us, event | category | flops | bytes accessed | tf_op | source)
XLA Modules:
  0.0 382.6 jit_solution(14501688388048622373)
XLA Ops:
  7.8 9.8 %all-to-all-start = ((s32[32,1,2]{2,1,0:T(1,128)}), s32[32,1,2]{2,1,0:T(1,128)}, u32[]{:S(2)}, u32[]{:S(2)}) async-start(s32[32,1,2]{2,1,0:T(1,128)} %bitcast), calls=%async_computation | async-start | bytes 32768 | tf_op jit(solution)/shard_map/all_to_all | solution.py:284
  37.3 7.4 %all-to-all-start.1 = ((bf16[32,2,20480]{2,1,0:T(2,128)(2,1)}), bf16[32,2,20480]{2,1,0:T(2,128)(2,1)S(1)}, u32[]{:S(2)}, u32[]{:S(2)}) async-start(bf16[32,2,20480]{2,1,0:T(2,128)(2,1)} %reshape.421), calls=%async_computation.1 | async-start | bytes 5242880 | tf_op jit(solution)/shard_map/all_to_all | solution.py:283
  70.1 10.0 %collective-permute-start.8 = (bf16[720,640]{1,0:T(8,128)(2,1)}, bf16[720,640]{1,0:T(8,128)(2,1)}, u32[]{:S(2)}, u32[]{:S(2)}) collective-permute-start(bf16[720,640]{1,0:T(8,128)(2,1)} %param.18), channel_id=1, source_target_pairs={{0,3},{1,0},{2,1},{3,2},{4,5},{5,6},{6,7},{7,4},{8,11},{9,8},{10,9... | collective-permute-start | bytes 2764808 | tf_op jit(solution)/shard_map/ppermute | solution.py:140
  118.4 4.9 %fusion.14 = f32[22,4,4,640]{3,0,2,1:T(8,128)S(1)} fusion(bf16[3,3,320,640]{3,2,1,0:T(8,128)(2,1)} %bitcast.1, bf16[22,8,8,320]{3,2,1,0:T(8,128)(2,1)S(1)} %reshape.423), kind=kOutput, calls=%fused_computation.45 | convolution fusion | flops 1090355200 | bytes 5488640 | tf_op jit(solution)/shard_map/conv_general_dilated | solution.py:17
  129.4 5.0 %multiply_reduce_fusion.2 = (f32[22,640]{1,0:T(8,128)S(1)}, f32[22,640]{1,0:T(8,128)S(1)}, f32[22,4,4,640]{3,0,2,1:T(8,128)S(1)}) fusion(f32[22,4]{0,1:T(4,128)S(1)} %fusion.50, f32[22,4,4,640]{3,0,2,1:T(8,128)S(1)} %fusion.14, bf16[3,3,320,640]{3,2,1,0:T(8,128)(2,1)} %bitcast.6, bf16[22,8,8,320]{3,2,1,0:T(8,128)(2,1)S(1)} %reshape.423), kind=kOutput, calls=%fused_computation.19 | convolution fusion | flops 1091228160 | bytes 6502752 | tf_op jit(solution)/shard_map/conv_general_dilated | solution.py:17
  149.9 12.3 %fusion.2 = bf16[22,8,8,320]{3,0,2,1:T(8,128)(2,1)S(1)} fusion(bf16[22,8,8,640]{3,0,2,1:T(8,128)(2,1)S(1)} %bitcast.109, bf16[3,3,640,320]{3,2,1,0:T(8,128)(2,1)} %bitcast.4, f32[22,8]{0,1:T(8,128)S(1)} %fusion.49, bf16[22,8,8,320]{3,2,1,0:T(8,128)(2,1)S(1)} %copy-done.8), kind=kOutput, calls=%fused_computation.8 | convolution fusion | flops 4363223040 | bytes 7291584 | tf_op jit(solution)/shard_map/conv_general_dilated | solution.py:17
  163.8 13.3 %multiply_convert_fusion = bf16[22,8,8,320]{3,0,2,1:T(8,128)(2,1)S(1)} fusion(bf16[22,8,8,320]{3,0,2,1:T(8,128)(2,1)S(1)} %fusion.2, bf16[22,8,8,640]{3,0,2,1:T(8,128)(2,1)S(1)} %bitcast.111, bf16[3,3,640,320]{3,2,1,0:T(8,128)(2,1)} %bitcast.9, bf16[22,8,8,320]{3,2,1,0:T(8,128)(2,1)S(1)} %copy-done.14, f32[22,8]{0,1:T(8,128)S(1)} %fusion.49, ...), kind=kOutput, calls=%fused_computation.11 | convolution fusion | flops 4367278080 | bytes 9093824 | tf_op jit(solution)/shard_map/conv_general_dilated | solution.py:17
  177.2 11.9 %fusion.56 = f32[3,3,640,320]{3,2,1,0:T(8,128)} fusion(bf16[22,8,8,640]{3,0,2,1:T(8,128)(2,1)S(1)} %bitcast.110, bf16[22,8,8,320]{3,0,2,1:T(8,128)(2,1)S(1)} %multiply_convert_fusion), kind=kOutput, calls=%fused_computation.163 | convolution fusion | flops 4361420800 | bytes 10076160 | tf_op jit(solution)/shard_map/conv_general_dilated | solution.py:29
  189.1 11.6 %fusion.55 = f32[22,8,8,640]{3,0,2,1:T(8,128)} fusion(bf16[22,8,8,320]{3,0,2,1:T(8,128)(2,1)S(1)} %multiply_convert_fusion, bf16[3,3,640,320]{3,2,1,0:T(8,128)(2,1)} %bitcast.4), kind=kOutput, calls=%fused_computation.162 | convolution fusion | flops 4361420800 | bytes 8192000 | tf_op jit(solution)/shard_map/conv_general_dilated | solution.py:17
  200.7 10.3 %concatenate.12 = f32[4,1,4,4,28800]{4,3,2,0,1:T(4,128)} reshape(f32[3,3,640,320]{3,2,1,0:T(8,128)} %fusion.56) | data formatting | bytes 14745600 | tf_op jit(solution)/shard_map/concatenate | solution.py:220
  223.5 3.7 mul.288
  227.2 7.4 %mul.289 = f32[22,4,4,640]{3,2,1,0:T(4,128)} reshape(f32[22,16,32,20]{3,2,1,0:T(8,128)} %mul.288) | data formatting | bytes 1802240 | tf_op jit(solution)/shard_map/mul | solution.py:78
  234.6 7.5 %fusion.12 = f32[3,3,320,640]{3,2,1,0:T(8,128)} fusion(bf16[22,8,8,320]{3,2,1,0:T(8,128)(2,1)S(1)} %copy-done.8, f32[22,4,4,640]{3,2,1,0:T(4,128)} %mul.289, f32[22,4,4,640]{3,0,2,1:T(8,128)S(1)} %fusion.14, f32[22,640]{1,0:T(8,128)S(1)} %copy-done.10, f32[22,640]{1,0:T(8,128)S(1)} %copy-done.11, f32[22,640]{1,0:T(8,128)S(1)} %mul.273, ...), kind=kOutput, calls=%fused_computation.43 | convolution fusion | flops 1093959680 | bytes 11202912 | tf_op jit(solution)/shard_map/conv_general_dilated | solution.py:29
  242.1 8.2 %concatenate.11 = f32[4,1,4,4,28800]{4,3,2,0,1:T(4,128)} reshape(f32[3,3,320,640]{3,2,1,0:T(8,128)} %fusion.12) | data formatting | bytes 14745600 | tf_op jit(solution)/shard_map/concatenate | solution.py:220
  250.3 6.7 %constant_dynamic-update-slice_fusion.21 = f32[4,2,4,4,28800]{4,3,2,0,1:T(4,128)} fusion(f32[4,1,4,4,28800]{4,3,2,0,1:T(4,128)} %concatenate.11), kind=kLoop, calls=%fused_computation.136 | loop fusion | bytes 14745600
  260.5 6.2 %fusion = bf16[4,4,4,28800]{3,2,1,0:T(4,128)(2,1)} fusion(f32[4,2,4,4,28800]{4,3,2,0,1:T(4,128)} %constant_dynamic-update-slice_fusion.20, s32[]{:T(128)S(6)} %select_n.248), kind=kLoop, calls=%fused_computation.4 | loop fusion | bytes 7372804 | tf_op jit(solution)/shard_map/convert_element_type | solution.py:193
  267.3 6.6 %collective-permute-done.16 = bf16[4,4,4,28800]{3,2,1,0:T(4,128)(2,1)} collective-permute-done((bf16[4,4,4,28800]{3,2,1,0:T(4,128)(2,1)}, bf16[4,4,4,28800]{3,2,1,0:T(4,128)(2,1)}, u32[]{:S(2)}, u32[]{:S(2)}) %collective-permute-start.16) | collective-permute-done | bytes 3686432 | tf_op jit(solution)/shard_map/ppermute | solution.py:193
  273.8 9.0 %bitcast_add_fusion = f32[4,4,4,28800]{3,2,1,0:T(4,128)} fusion(bf16[4,4,4,28800]{3,2,1,0:T(4,128)(2,1)} %collective-permute-done.16, f32[4,2,4,4,28800]{4,3,2,0,1:T(4,128)} %constant_dynamic-update-slice_fusion.20, s32[]{:T(128)S(6)} %select_n.246), kind=kLoop, calls=%fused_computation.2 | loop fusion | flops 3686400 | bytes 18432004 | tf_op jit(solution)/shard_map/add | solution.py:194
  282.9 5.3 %fusion.54 = (f32[4,4,4,14400]{3,2,1,0:T(4,128)S(1)}, f32[4,4,4,14400]{3,2,1,0:T(4,128)S(1)}) fusion(f32[4,4,4,28800]{3,2,1,0:T(4,128)} %bitcast_add_fusion), kind=kLoop, calls=%fused_computation.161 | loop fusion | bytes 14745600 | tf_op jit(solution)/shard_map/slice | solution.py:232
  297.7 4.2 %collective-permute-done.17 = bf16[4,4,14400]{2,1,0:T(4,128)(2,1)S(1)} collective-permute-done((bf16[4,4,14400]{2,1,0:T(4,128)(2,1)S(1)}, bf16[4,4,14400]{2,1,0:T(4,128)(2,1)S(1)}, u32[]{:S(2)}, u32[]{:S(2)}) %collective-permute-start.17) | collective-permute-done | bytes 460832 | tf_op jit(solution)/shard_map/ppermute | solution.py:193
  305.0 6.9 %collective-permute-done.18 = bf16[4,4,14400]{2,1,0:T(4,128)(2,1)S(1)} collective-permute-done((bf16[4,4,14400]{2,1,0:T(4,128)(2,1)S(1)}, bf16[4,4,14400]{2,1,0:T(4,128)(2,1)S(1)}, u32[]{:S(2)}, u32[]{:S(2)}) %collective-permute-start.18) | collective-permute-done | bytes 460832 | tf_op jit(solution)/shard_map/ppermute | solution.py:193
  350.7 5.3 %collective-permute-done.35 = bf16[4,28800]{1,0:T(4,128)(2,1)S(1)} collective-permute-done((bf16[4,28800]{1,0:T(4,128)(2,1)S(1)}, bf16[4,28800]{1,0:T(4,128)(2,1)S(1)}, u32[]{:S(2)}, u32[]{:S(2)}) %collective-permute-start.35) | collective-permute-done | bytes 230432 | tf_op jit(solution)/shard_map/ppermute | solution.py:202
  356.7 12.5 %collective-permute-start.38 = (bf16[4,4,28800]{2,1,0:T(4,128)(2,1)S(1)}, bf16[4,4,28800]{2,1,0:T(4,128)(2,1)S(1)}, u32[]{:S(2)}, u32[]{:S(2)}) collective-permute-start(bf16[4,4,28800]{2,1,0:T(4,128)(2,1)S(1)} %bitcast_dynamic-update-slice_fusion.2), channel_id=1, source_target_pairs={{0,4},{1,5},{2,6},{3,7},{4,0},{5,1},{6,2},{7,3},{8,12},{9,13},{10,... | collective-permute-start | bytes 2764808 | tf_op jit(solution)/shard_map/ppermute | solution.py:202
  378.8 3.7 reshape.435
  (248 shorter events, 191.3 us)
Async XLA Ops:
  0.6 46.5 %collective-permute-start.4 = (bf16[1440,320]{0,1:T(8,128)(2,1)}, bf16[1440,320]{0,1:T(8,128)(2,1)}, u32[]{:S(2)}, u32[]{:S(2)}) collective-permute-start(bf16[1440,320]{0,1:T(8,128)(2,1)} %param.17), channel_id=1, source_target_pairs={{0,3},{1,0},{2,1},{3,2},{4,5},{5,6},{6,7},{7,4},{8,11},{9,8},{10,9... | collective-permute-start | bytes 2764808 | tf_op jit(solution)/shard_map/ppermute | solution.py:140
  2.8 46.7 %collective-permute-start = (bf16[720,640]{1,0:T(8,128)(2,1)}, bf16[720,640]{1,0:T(8,128)(2,1)}, u32[]{:S(2)}, u32[]{:S(2)}) collective-permute-start(bf16[720,640]{1,0:T(8,128)(2,1)} %param.16), channel_id=1, source_target_pairs={{0,3},{1,0},{2,1},{3,2},{4,5},{5,6},{6,7},{7,4},{8,11},{9,8},{10,9... | collective-permute-start | bytes 2764808 | tf_op jit(solution)/shard_map/ppermute | solution.py:140
  7.8 29.4 %all-to-all-start = ((s32[32,1,2]{2,1,0:T(1,128)}), s32[32,1,2]{2,1,0:T(1,128)}, u32[]{:S(2)}, u32[]{:S(2)}) async-start(s32[32,1,2]{2,1,0:T(1,128)} %bitcast), calls=%async_computation | async-start | bytes 32768 | tf_op jit(solution)/shard_map/all_to_all | solution.py:284
  37.3 74.5 %all-to-all-start.1 = ((bf16[32,2,20480]{2,1,0:T(2,128)(2,1)}), bf16[32,2,20480]{2,1,0:T(2,128)(2,1)S(1)}, u32[]{:S(2)}, u32[]{:S(2)}) async-start(bf16[32,2,20480]{2,1,0:T(2,128)(2,1)} %reshape.421), calls=%async_computation.1 | async-start | bytes 5242880 | tf_op jit(solution)/shard_map/all_to_all | solution.py:283
  49.5 20.6 %collective-permute-start.5 = (bf16[1440,320]{0,1:T(8,128)(2,1)}, bf16[1440,320]{0,1:T(8,128)(2,1)}, u32[]{:S(2)}, u32[]{:S(2)}) collective-permute-start(bf16[1440,320]{0,1:T(8,128)(2,1)} %collective-permute-done.4), channel_id=1, source_target_pairs={{0,4},{4,0},{8,12},{12,8},{16,20},{20,16},{24,28},{28,24},{32,36},... | collective-permute-start | bytes 2764808 | tf_op jit(solution)/shard_map/ppermute | solution.py:147
  51.3 11.3 %collective-permute-start.2 = (bf16[360,640]{1,0:T(8,128)(2,1)}, bf16[360,640]{1,0:T(8,128)(2,1)}, u32[]{:S(2)}, u32[]{:S(2)}) collective-permute-start(bf16[360,640]{1,0:T(8,128)(2,1)} %constant_dynamic-slice_fusion.3), channel_id=1, source_target_pairs={{0,3},{1,0},{2,1},{3,2},{4,5},{5,6},{6,7},{7,4},{8,11},{9,8},{10,9... | collective-permute-start | bytes 1382408 | tf_op jit(solution)/shard_map/ppermute | solution.py:145
  52.3 37.7 %collective-permute-start.1 = (bf16[720,640]{1,0:T(8,128)(2,1)}, bf16[720,640]{1,0:T(8,128)(2,1)}, u32[]{:S(2)}, u32[]{:S(2)}) collective-permute-start(bf16[720,640]{1,0:T(8,128)(2,1)} %collective-permute-done), channel_id=1, source_target_pairs={{0,4},{4,0},{8,12},{12,8},{16,20},{20,16},{24,28},{28,24},{32,36},... | collective-permute-start | bytes 2764808 | tf_op jit(solution)/shard_map/ppermute | solution.py:147
  59.2 28.8 %collective-permute-start.7 = (bf16[720,320]{0,1:T(8,128)(2,1)}, bf16[720,320]{0,1:T(8,128)(2,1)}, u32[]{:S(2)}, u32[]{:S(2)}) collective-permute-start(bf16[720,320]{0,1:T(8,128)(2,1)} %collective-permute-done.6), channel_id=1, source_target_pairs={{0,4},{4,0},{8,12},{12,8},{16,20},{20,16},{24,28},{28,24},{32,36},... | collective-permute-start | bytes 1382408 | tf_op jit(solution)/shard_map/ppermute | solution.py:147
  64.9 33.1 %collective-permute-start.12 = (bf16[1440,320]{0,1:T(8,128)(2,1)}, bf16[1440,320]{0,1:T(8,128)(2,1)}, u32[]{:S(2)}, u32[]{:S(2)}) collective-permute-start(bf16[1440,320]{0,1:T(8,128)(2,1)} %param.19), channel_id=1, source_target_pairs={{0,3},{1,0},{2,1},{3,2},{4,5},{5,6},{6,7},{7,4},{8,11},{9,8},{10,9... | collective-permute-start | bytes 2764808 | tf_op jit(solution)/shard_map/ppermute | solution.py:140
  64.9 29.3 %collective-permute-start.3 = (bf16[360,640]{1,0:T(8,128)(2,1)}, bf16[360,640]{1,0:T(8,128)(2,1)}, u32[]{:S(2)}, u32[]{:S(2)}) collective-permute-start(bf16[360,640]{1,0:T(8,128)(2,1)} %collective-permute-done.2), channel_id=1, source_target_pairs={{0,4},{4,0},{8,12},{12,8},{16,20},{20,16},{24,28},{28,24},{32,36},... | collective-permute-start | bytes 1382408 | tf_op jit(solution)/shard_map/ppermute | solution.py:147
  70.1 31.0 %collective-permute-start.8 = (bf16[720,640]{1,0:T(8,128)(2,1)}, bf16[720,640]{1,0:T(8,128)(2,1)}, u32[]{:S(2)}, u32[]{:S(2)}) collective-permute-start(bf16[720,640]{1,0:T(8,128)(2,1)} %param.18), channel_id=1, source_target_pairs={{0,3},{1,0},{2,1},{3,2},{4,5},{5,6},{6,7},{7,4},{8,11},{9,8},{10,9... | collective-permute-start | bytes 2764808 | tf_op jit(solution)/shard_map/ppermute | solution.py:140
  100.1 23.2 %collective-permute-start.14 = (bf16[720,320]{0,1:T(8,128)(2,1)}, bf16[720,320]{0,1:T(8,128)(2,1)}, u32[]{:S(2)}, u32[]{:S(2)}) collective-permute-start(bf16[720,320]{0,1:T(8,128)(2,1)} %constant_dynamic-slice_fusion), channel_id=1, source_target_pairs={{0,3},{1,0},{2,1},{3,2},{4,5},{5,6},{6,7},{7,4},{8,11},{9,8},{10,9... | collective-permute-start | bytes 1382408 | tf_op jit(solution)/shard_map/ppermute | solution.py:145
  102.9 14.9 %collective-permute-start.10 = (bf16[360,640]{1,0:T(8,128)(2,1)}, bf16[360,640]{1,0:T(8,128)(2,1)}, u32[]{:S(2)}, u32[]{:S(2)}) collective-permute-start(bf16[360,640]{1,0:T(8,128)(2,1)} %constant_dynamic-slice_fusion.1), channel_id=1, source_target_pairs={{0,3},{1,0},{2,1},{3,2},{4,5},{5,6},{6,7},{7,4},{8,11},{9,8},{10,9... | collective-permute-start | bytes 1382408 | tf_op jit(solution)/shard_map/ppermute | solution.py:145
  106.1 19.6 %collective-permute-start.9 = (bf16[720,640]{1,0:T(8,128)(2,1)}, bf16[720,640]{1,0:T(8,128)(2,1)S(1)}, u32[]{:S(2)}, u32[]{:S(2)}) collective-permute-start(bf16[720,640]{1,0:T(8,128)(2,1)} %collective-permute-done.8), channel_id=1, source_target_pairs={{0,4},{4,0},{8,12},{12,8},{16,20},{20,16},{24,28},{28,24},{32,36},... | collective-permute-start | bytes 2764808 | tf_op jit(solution)/shard_map/ppermute | solution.py:147
  109.6 28.2 %collective-permute-start.13 = (bf16[1440,320]{0,1:T(8,128)(2,1)}, bf16[1440,320]{0,1:T(8,128)(2,1)}, u32[]{:S(2)}, u32[]{:S(2)}) collective-permute-start(bf16[1440,320]{0,1:T(8,128)(2,1)} %collective-permute-done.12), channel_id=1, source_target_pairs={{0,4},{4,0},{8,12},{12,8},{16,20},{20,16},{24,28},{28,24},{32,36},... | collective-permute-start | bytes 2764808 | tf_op jit(solution)/shard_map/ppermute | solution.py:147
  117.8 10.8 %collective-permute-start.11 = (bf16[360,640]{1,0:T(8,128)(2,1)}, bf16[360,640]{1,0:T(8,128)(2,1)S(1)}, u32[]{:S(2)}, u32[]{:S(2)}) collective-permute-start(bf16[360,640]{1,0:T(8,128)(2,1)} %collective-permute-done.10), channel_id=1, source_target_pairs={{0,4},{4,0},{8,12},{12,8},{16,20},{20,16},{24,28},{28,24},{32,36},... | collective-permute-start | bytes 1382408 | tf_op jit(solution)/shard_map/ppermute | solution.py:147
  125.4 20.6 %collective-permute-start.15 = (bf16[720,320]{0,1:T(8,128)(2,1)}, bf16[720,320]{0,1:T(8,128)(2,1)}, u32[]{:S(2)}, u32[]{:S(2)}) collective-permute-start(bf16[720,320]{0,1:T(8,128)(2,1)} %collective-permute-done.14), channel_id=1, source_target_pairs={{0,4},{4,0},{8,12},{12,8},{16,20},{20,16},{24,28},{28,24},{32,36},... | collective-permute-start | bytes 1382408 | tf_op jit(solution)/shard_map/ppermute | solution.py:147
  288.7 13.3 %collective-permute-start.17 = (bf16[4,4,14400]{2,1,0:T(4,128)(2,1)S(1)}, bf16[4,4,14400]{2,1,0:T(4,128)(2,1)S(1)}, u32[]{:S(2)}, u32[]{:S(2)}) collective-permute-start(bf16[4,4,14400]{2,1,0:T(4,128)(2,1)S(1)} %get-tuple-element.35), channel_id=1, source_target_pairs={{0,1},{1,2},{2,3},{3,0},{4,5},{5,6},{6,7},{7,4},{8,9},{9,10},{10,1... | collective-permute-start | bytes 1382408 | tf_op jit(solution)/shard_map/ppermute | solution.py:193
  289.5 22.4 %collective-permute-start.18 = (bf16[4,4,14400]{2,1,0:T(4,128)(2,1)S(1)}, bf16[4,4,14400]{2,1,0:T(4,128)(2,1)S(1)}, u32[]{:S(2)}, u32[]{:S(2)}) collective-permute-start(bf16[4,4,14400]{2,1,0:T(4,128)(2,1)S(1)} %get-tuple-element.37), channel_id=1, source_target_pairs={{0,2},{1,3},{2,0},{3,1},{4,6},{5,7},{6,4},{7,5},{8,10},{9,11},{10,... | collective-permute-start | bytes 1382408 | tf_op jit(solution)/shard_map/ppermute | solution.py:193
  291.4 20.8 %collective-permute-start.19 = (bf16[4,4,14400]{2,1,0:T(4,128)(2,1)S(1)}, bf16[4,4,14400]{2,1,0:T(4,128)(2,1)S(1)}, u32[]{:S(2)}, u32[]{:S(2)}) collective-permute-start(bf16[4,4,14400]{2,1,0:T(4,128)(2,1)S(1)} %get-tuple-element.36), channel_id=1, source_target_pairs={{0,3},{1,0},{2,1},{3,2},{4,7},{5,4},{6,5},{7,6},{8,11},{9,8},{10,9... | collective-permute-start | bytes 1382408 | tf_op jit(solution)/shard_map/ppermute | solution.py:193
  293.8 23.0 %collective-permute-start.23 = (bf16[4,4,14400]{2,1,0:T(4,128)(2,1)S(1)}, bf16[4,4,14400]{2,1,0:T(4,128)(2,1)S(1)}, u32[]{:S(2)}, u32[]{:S(2)}) collective-permute-start(bf16[4,4,14400]{2,1,0:T(4,128)(2,1)S(1)} %get-tuple-element.38), channel_id=1, source_target_pairs={{0,32},{1,33},{2,34},{3,35},{4,36},{5,37},{6,38},{7,39},{8,40},{9,... | collective-permute-start | bytes 1382408 | tf_op jit(solution)/shard_map/ppermute | solution.py:193
  295.3 22.7 %collective-permute-start.24 = (bf16[4,4,14400]{2,1,0:T(4,128)(2,1)S(1)}, bf16[4,4,14400]{2,1,0:T(4,128)(2,1)S(1)}, u32[]{:S(2)}, u32[]{:S(2)}) collective-permute-start(bf16[4,4,14400]{2,1,0:T(4,128)(2,1)S(1)} %get-tuple-element.40), channel_id=1, source_target_pairs={{0,64},{1,65},{2,66},{3,67},{4,68},{5,69},{6,70},{7,71},{8,72},{9,... | collective-permute-start | bytes 1382408 | tf_op jit(solution)/shard_map/ppermute | solution.py:193
  302.0 16.0 %collective-permute-start.25 = (bf16[4,4,14400]{2,1,0:T(4,128)(2,1)S(1)}, bf16[4,4,14400]{2,1,0:T(4,128)(2,1)S(1)}, u32[]{:S(2)}, u32[]{:S(2)}) collective-permute-start(bf16[4,4,14400]{2,1,0:T(4,128)(2,1)S(1)} %get-tuple-element.39), channel_id=1, source_target_pairs={{0,96},{1,97},{2,98},{3,99},{4,100},{5,101},{6,102},{7,103},{8,104... | collective-permute-start | bytes 1382408 | tf_op jit(solution)/shard_map/ppermute | solution.py:193
  356.7 14.6 %collective-permute-start.38 = (bf16[4,4,28800]{2,1,0:T(4,128)(2,1)S(1)}, bf16[4,4,28800]{2,1,0:T(4,128)(2,1)S(1)}, u32[]{:S(2)}, u32[]{:S(2)}) collective-permute-start(bf16[4,4,28800]{2,1,0:T(4,128)(2,1)S(1)} %bitcast_dynamic-update-slice_fusion.2), channel_id=1, source_target_pairs={{0,4},{1,5},{2,6},{3,7},{4,0},{5,1},{6,2},{7,3},{8,12},{9,13},{10,... | collective-permute-start | bytes 2764808 | tf_op jit(solution)/shard_map/ppermute | solution.py:202
  (34 other events, 236.7 us)
